TPU v7x, 128 devices: a whole 4x4x4 slice. The times are simulated.
128 devices in a mesh: px: 8 (over z, core), py: 16 (over y, x).
Axes of the slice: x: 4, y: 4, z: 4, core: 2. Of those that a mesh axis runs over, the one named last changes fastest.
Arguments:
- fractions: float32 [4096, 3, 128], P(('px', 'py')), may hold values from 0 to 1
- charge: float32 [4096, 128], P(('px', 'py')), may hold values from -4 to 4
- cell_index: int32 [4096, 128], P(('px', 'py')), may hold values from 0 to 131071
- destination: int32 [4096, 1], P(('px', 'py')), may hold values from 0 to 15; in each aligned block of 32 rows (0 to 31, 32 to 63, ...) at most 3 rows name the same one
- live_blocks: int32 [128], P(('px', 'py')), may hold values from 16 to 32, as said below
Outputs:
- forces: float32 [4096, 3, 128], P(('px', 'py'))
Inputs may be any that keep to these rules, and one draw needn't show every extreme that they name: `destination`: in the rows of one device no value is named by more than 3 blocks, a bound that some block reaches. `live_blocks`: some domain has all 32 slots occupied in every draw.
All inputs are finite; a program needn't handle non-finite values.
Results may differ from a plain program's by a relative error of at most 0.0003.
Values sent between devices are 32-bit elements; how exact they have to be, the bound alone decides.
No kernel may reach another device: no remote copies, remote signals or barrier semaphores. Data moves between devices by JAX's collectives and lax.ppermute only.
A program may use at most 128 MiB of HBM per device.

v0:
```python
import math

import jax
import jax.numpy as jnp
from jax import lax
from jax.sharding import PartitionSpec as P

K = 256


EWALD_GAIN = 4.0
EWALD_BETA = 0.6
SPLINE_SUMS = (1.0 / 120.0, 26.0 / 120.0, 66.0 / 120.0, 26.0 / 120.0, 1.0 / 120.0)
HIGHEST = lax.Precision.HIGHEST


def swapped(block, axis, bit):
    count = lax.axis_size(axis)
    route = []
    for low in range(count):
        high = low | 1 << bit
        if high != low and high < count:
            route += [(low, high), (high, low)]
    return lax.ppermute(block, axis, route)


def from_behind(value, axis, steps):
    count = lax.axis_size(axis)
    pairs = [(source, (source + steps) % count) for source in range(count)]
    return lax.ppermute(value, axis, pairs)


def spline_six(u):
    older_values = [1.0 - u, u]
    slopes = []
    for spline_order in range(3, 7):
        newer_values = []
        for k in range(spline_order):
            from_left = older_values[k - 1] if k >= 1 else jnp.zeros_like(u)
            from_right = older_values[k] if k <= spline_order - 2 else jnp.zeros_like(u)
            newer_values.append(
                ((u + (spline_order - 1 - k)) * from_left + (k + 1 - u) * from_right)
                * (1.0 / (spline_order - 1))
            )
        if spline_order == 6:
            slopes = [
                (older_values[k - 1] if k >= 1 else jnp.zeros_like(u))
                - (older_values[k] if k <= 4 else jnp.zeros_like(u))
                for k in range(6)
            ]
        older_values = newer_values
    return (older_values, slopes)


def modulus(wave, extent):
    cos_sum = jnp.zeros(wave.shape, jnp.float32)
    sin_sum = jnp.zeros(wave.shape, jnp.float32)
    for j, value in enumerate(SPLINE_SUMS):
        angle = 2.0 * math.pi / extent * (wave * j % extent).astype(jnp.float32)
        cos_sum = cos_sum + value * jnp.cos(angle)
        sin_sum = sin_sum + value * jnp.sin(angle)
    return 1.0 / (cos_sum * cos_sum + sin_sum * sin_sum)


def influence(wave_x, wave_y, wave_z, extent):
    folded_x = jnp.where(2 * wave_x < extent, wave_x, wave_x - extent).astype(jnp.float32) / extent
    folded_y = jnp.where(2 * wave_y < extent, wave_y, wave_y - extent).astype(jnp.float32) / extent
    folded_z = jnp.where(2 * wave_z < extent, wave_z, wave_z - extent).astype(jnp.float32) / extent
    squared = folded_x * folded_x + folded_y * folded_y + folded_z * folded_z
    safe_squared = jnp.where(squared > 0, squared, 1.0)
    value = (
        EWALD_GAIN
        * jnp.exp(-(math.pi * math.pi) * squared / (EWALD_BETA * EWALD_BETA))
        / safe_squared
    )
    value = value * modulus(wave_x, extent) * modulus(wave_y, extent) * modulus(wave_z, extent)
    return jnp.where(squared > 0, value, 0.0)


def wave_tables(extent):
    steps = jnp.arange(extent, dtype=jnp.int32)
    product = steps[:, None] * steps[None, :] % extent
    angle = 2.0 * math.pi / extent * product.astype(jnp.float32)
    return (jnp.cos(angle), jnp.sin(angle))


def local_forward(start, count, parts):
    outputs = jnp.arange(count, dtype=jnp.int32)[:, None]
    inputs = jnp.arange(count, dtype=jnp.int32)[None, :]
    total = parts * count
    product = inputs * (start + parts * outputs) % total
    angle = -2.0 * math.pi / total * product.astype(jnp.float32)
    return (jnp.cos(angle), jnp.sin(angle))


def reverse_bits(index, count_bits):
    result = jnp.zeros((), jnp.int32)
    for b in range(count_bits):
        result = result + ((index >> b & 1) << count_bits - 1 - b)
    return result


def mix_rows(spectrum, mat_cos, mat_sin):

    def apply_matrix(matrix, values):
        return jnp.einsum("sm,myz->syz", matrix, values, precision=HIGHEST)

    real_part, imag_part = (spectrum[0], spectrum[1])
    return jnp.stack(
        [
            apply_matrix(mat_cos, real_part) - apply_matrix(mat_sin, imag_part),
            apply_matrix(mat_cos, imag_part) + apply_matrix(mat_sin, real_part),
        ]
    )


def mix_columns(spectrum, mat_cos, mat_sin):

    def apply_matrix(matrix, values):
        return jnp.einsum("sm,xmz->xsz", matrix, values, precision=HIGHEST)

    real_part, imag_part = (spectrum[0], spectrum[1])
    return jnp.stack(
        [
            apply_matrix(mat_cos, real_part) - apply_matrix(mat_sin, imag_part),
            apply_matrix(mat_cos, imag_part) + apply_matrix(mat_sin, real_part),
        ]
    )


def swap_rows(spectrum, bit_number):
    return swapped(spectrum, "px", bit_number)


def swap_columns(spectrum, bit_number):
    return swapped(spectrum, "py", bit_number)


def butterfly_section(spectrum, index, bit_number, inverse, exchanger):
    upper = index >> bit_number & 1 == 1
    lower = (index & (1 << bit_number) - 1).astype(jnp.float32)
    angle = -2.0 * math.pi / 2 ** (bit_number + 1) * lower
    turn_cos = jnp.cos(angle)
    turn_sin = jnp.sin(angle)
    real_part, imag_part = (spectrum[0], spectrum[1])
    if inverse:
        turned = jnp.stack(
            [
                turn_cos * real_part + turn_sin * imag_part,
                turn_cos * imag_part - turn_sin * real_part,
            ]
        )
        own_value = jnp.where(upper, turned, spectrum)
        partner = exchanger(own_value, bit_number)
        return jnp.where(upper, partner - own_value, own_value + partner)
    partner = exchanger(spectrum, bit_number)
    diff_real = partner[0] - real_part
    diff_imag = partner[1] - imag_part
    turned = jnp.stack(
        [turn_cos * diff_real - turn_sin * diff_imag, turn_sin * diff_real + turn_cos * diff_imag]
    )
    return jnp.where(upper, turned, spectrum + partner)


def place_table(base, values, span):
    atoms_count = base.shape[0]
    slots_index = jnp.arange(span, dtype=jnp.int32)[:, None]
    table = jnp.zeros((span, atoms_count), jnp.float32)
    for k in range(6):
        table = table + jnp.where(slots_index == (base + k)[None, :], values[k][None, :], 0.0)
    return table


def place_depth(base, values, extent):
    depth_index = jnp.arange(extent, dtype=jnp.int32)[None, :]
    table = jnp.zeros((base.shape[0], extent), jnp.float32)
    for k in range(6):
        table = table + jnp.where(
            depth_index == ((base + k) % extent)[:, None], values[k][:, None], 0.0
        )
    return table


def per_device(fractions, charge, cell_index, destination, live_blocks):
    rows_dev = lax.axis_size("px")
    cols_dev = lax.axis_size("py")
    span_x = K // rows_dev
    span_y = K // cols_dev
    blocks = charge.shape[0]
    width = charge.shape[1]
    capacity = max(2, 3 * blocks // (2 * cols_dev))
    slots = cols_dev * capacity
    group_blocks = 4
    groups = slots // group_blocks
    atoms_group = group_blocks * width
    alive = (jnp.arange(blocks, dtype=jnp.int32) < live_blocks[0]).astype(jnp.float32)
    target = destination[:, 0]
    matches = (target[:, None] == jnp.arange(cols_dev, dtype=jnp.int32)[None, :]).astype(jnp.int32)
    earlier = jnp.cumsum(matches, axis=0) - matches
    position = jnp.sum(earlier * matches, axis=1)
    slot_of = target * capacity + position
    picked = (slot_of[None, :] == jnp.arange(slots, dtype=jnp.int32)[:, None]).astype(jnp.int32)
    source_block = jnp.sum(picked * jnp.arange(blocks, dtype=jnp.int32)[None, :], axis=1)
    used = jnp.sum(picked, axis=1).astype(jnp.float32)
    payload = jnp.concatenate(
        [
            fractions,
            (charge * alive[:, None])[:, None, :],
            cell_index.astype(jnp.float32)[:, None, :],
        ],
        axis=1,
    )
    outgoing = (jnp.take(payload, source_block, axis=0) * used[:, None, None]).reshape(
        cols_dev, capacity, 5, width
    )
    arrived = lax.all_to_all(outgoing, "py", split_axis=0, concat_axis=0, tiled=True)
    grouped = (
        arrived.reshape(groups, group_blocks, 5, width)
        .transpose(0, 2, 1, 3)
        .reshape(groups, 5, atoms_group)
    )

    def deposit(charge_grid, group):
        cell_value = group[4].astype(jnp.int32)
        base_x = cell_value // (span_y * K)
        base_y = cell_value // K % span_y
        base_z = cell_value % K
        splines_x, slopes_x = spline_six(group[0])
        splines_y, slopes_y = spline_six(group[1])
        splines_z, slopes_z = spline_six(group[2])
        table_x = place_table(base_x, splines_x, span_x + 5)
        slope_x = place_table(base_x, slopes_x, span_x + 5)
        table_y = place_table(base_y, splines_y, span_y + 5)
        slope_y = place_table(base_y, slopes_y, span_y + 5)
        table_z = place_depth(base_z, splines_z, K)
        slope_z = place_depth(base_z, slopes_z, K)
        outer_table = (table_x[:, None, :] * table_y[None, :, :]).reshape(-1, atoms_group)
        charge_grid = charge_grid + jnp.dot(
            outer_table, table_z * group[3][:, None], precision=HIGHEST
        )
        return (charge_grid, (table_x, slope_x, table_y, slope_y, table_z, slope_z, group[3]))

    start_grid = jnp.zeros(((span_x + 5) * (span_y + 5), K), jnp.float32)
    extended, stored = lax.scan(deposit, start_grid, grouped)
    extended = extended.reshape(span_x + 5, span_y + 5, K)
    moved_rows = from_behind(extended[span_x:], "px", 1)
    extended = jnp.concatenate([extended[:5] + moved_rows, extended[5:span_x]], axis=0)
    moved_cols = from_behind(extended[:, span_y:], "py", 1)
    charge_grid = jnp.concatenate([extended[:, :5] + moved_cols, extended[:, 5:span_y]], axis=1)
    depth_cos, depth_sin = wave_tables(K)
    flat_grid = charge_grid.reshape(span_x * span_y, K)
    spectrum = jnp.stack(
        [
            jnp.dot(flat_grid, depth_cos, precision=HIGHEST),
            -jnp.dot(flat_grid, depth_sin, precision=HIGHEST),
        ]
    ).reshape(2, span_x, span_y, K)
    index_x = lax.axis_index("px")
    index_y = lax.axis_index("py")
    bits_x = rows_dev.bit_length() - 1
    bits_y = cols_dev.bit_length() - 1
    start_x = reverse_bits(index_x, bits_x)
    start_y = reverse_bits(index_y, bits_y)
    for bit_number in reversed(range(bits_y)):
        spectrum = butterfly_section(spectrum, index_y, bit_number, False, swap_columns)
    column_cos, column_sin = local_forward(start_y, span_y, cols_dev)
    spectrum = mix_columns(spectrum, column_cos, column_sin)
    wave_y = start_y + cols_dev * jnp.arange(span_y, dtype=jnp.int32)
    wave_z = jnp.arange(K, dtype=jnp.int32)
    for bit_number in reversed(range(bits_x)):
        spectrum = butterfly_section(spectrum, index_x, bit_number, False, swap_rows)
    row_cos, row_sin = local_forward(start_x, span_x, rows_dev)
    spectrum = mix_rows(spectrum, row_cos, row_sin)
    wave_x = start_x + rows_dev * jnp.arange(span_x, dtype=jnp.int32)
    kernel = influence(wave_x[:, None, None], wave_y[None, :, None], wave_z[None, None, :], K) * (
        1.0 / float(K**3)
    )
    spectrum = spectrum * kernel[None]
    spectrum = mix_rows(spectrum, row_cos.T, -row_sin.T)
    for bit_number in range(bits_x):
        spectrum = butterfly_section(spectrum, index_x, bit_number, True, swap_rows)
    spectrum = mix_columns(spectrum, column_cos.T, -column_sin.T)
    for bit_number in range(bits_y):
        spectrum = butterfly_section(spectrum, index_y, bit_number, True, swap_columns)
    real_flat = spectrum[0].reshape(span_x * span_y, K)
    imag_flat = spectrum[1].reshape(span_x * span_y, K)
    potential = (
        jnp.dot(real_flat, depth_cos, precision=HIGHEST)
        - jnp.dot(imag_flat, depth_sin, precision=HIGHEST)
    ).reshape(span_x, span_y, K)
    lower_rows = from_behind(potential[:5], "px", -1)
    potential = jnp.concatenate([potential, lower_rows], axis=0)
    lower_cols = from_behind(potential[:, :5], "py", -1)
    potential = jnp.concatenate([potential, lower_cols], axis=1).reshape(-1, K)

    def pull(carry, tables):
        table_x, slope_x, table_y, slope_y, table_z, slope_z, amounts = tables
        stacked = jnp.stack(
            [
                table_x[:, None, :] * table_y[None, :, :],
                slope_x[:, None, :] * table_y[None, :, :],
                table_x[:, None, :] * slope_y[None, :, :],
            ]
        ).reshape(3, -1, atoms_group)
        sampled = jnp.einsum("cga,gz->caz", stacked, potential, precision=HIGHEST)
        force_x = -amounts * jnp.sum(sampled[1] * table_z, axis=1)
        force_y = -amounts * jnp.sum(sampled[2] * table_z, axis=1)
        force_z = -amounts * jnp.sum(sampled[0] * slope_z, axis=1)
        return (carry, jnp.stack([force_x, force_y, force_z]))

    _, pulled = lax.scan(pull, jnp.zeros((), jnp.float32), stored)
    pulled = (
        pulled.reshape(groups, 3, group_blocks, width)
        .transpose(0, 2, 1, 3)
        .reshape(cols_dev, capacity, 3, width)
    )
    returned = lax.all_to_all(pulled, "py", split_axis=0, concat_axis=0, tiled=True).reshape(
        slots, 3, width
    )
    return jnp.take(returned, slot_of, axis=0) * alive[:, None, None]


def solution(mesh):
    placed = (
        P(("px", "py"), None, None),
        P(("px", "py"), None),
        P(("px", "py"), None),
        P(("px", "py"), None),
        P(("px", "py")),
    )
    return jax.shard_map(
        per_device,
        mesh=mesh,
        in_specs=placed,
        out_specs=P(("px", "py"), None, None),
        check_vma=False,
    )
```

profile of v0, /device:TPU:0, one launch (start us, length us, event | category | flops | bytes accessed | tf_op | source)
XLA Modules:
  0.0 888.8 jit_solution(3755770130116577499)
XLA Ops:
  7.1 7.1 all-to-all-start
  14.3 8.1 all-to-all-done
  23.3 235.7 %while.39 = (s32[]{:T(128)}, f32[777,256]{1,0:T(8,128)}, f32[12,37,512]{2,1,0:T(8,128)}, f32[12,37,512]{2,1,0:T(8,128)}, f32[12,21,512]{2,1,0:T(8,128)}, /*index...) while((s32[]{:T(128)}, f32[777,256]{1,0:T(8,128)}, ...), condition=%wide.region_5.6_spmd.clone, body=%wide.region_4.5_spmd.clone.sunk | while | flops 1231531008 | bytes 10090179 | solution.py:244
  266.2 9.4 %collective-permute-done.1 = f32[32,5,256]{2,1,0:T(8,128)S(1)} collective-permute-done((f32[32,5,256]{2,1,0:T(8,128)S(1)}, f32[32,5,256]{2,1,0:T(8,128)S(1)}, u32[]{:S(2)}, u32[]{:S(2)}) %collective-permute-start.1) | collective-permute-done | bytes 163872 | tf_op jit(solution)/shard_map/ppermute | solution.py:30
  279.1 23.9 %collective-permute-done.2 = f32[2,32,16,256]{3,2,1,0:T(8,128)S(1)} collective-permute-done((f32[2,32,16,256]{3,2,1,0:T(8,128)S(1)}, f32[2,32,16,256]{3,2,1,0:T(8,128)S(1)}, u32[]{:S(2)}, u32[]{:S(2)}) %collective-permute-start.2) | collective-permute-done | bytes 1048608 | tf_op jit(solution)/shard_map/ppermute | solution.py:24
  304.9 21.9 %collective-permute-done.3 = f32[2,32,16,256]{3,2,1,0:T(8,128)} collective-permute-done((f32[2,32,16,256]{3,2,1,0:T(8,128)}, f32[2,32,16,256]{3,2,1,0:T(8,128)}, u32[]{:S(2)}, u32[]{:S(2)}) %collective-permute-start.3) | collective-permute-done | bytes 1048608 | tf_op jit(solution)/shard_map/ppermute | solution.py:24
  330.8 25.1 %collective-permute-done.4 = f32[2,32,16,256]{3,2,1,0:T(8,128)S(1)} collective-permute-done((f32[2,32,16,256]{3,2,1,0:T(8,128)S(1)}, f32[2,32,16,256]{3,2,1,0:T(8,128)S(1)}, u32[]{:S(2)}, u32[]{:S(2)}) %collective-permute-start.4) | collective-permute-done | bytes 1048608 | tf_op jit(solution)/shard_map/ppermute | solution.py:24
  356.7 17.1 %collective-permute-done.5 = f32[2,32,16,256]{3,2,1,0:T(8,128)S(1)} collective-permute-done((f32[2,32,16,256]{3,2,1,0:T(8,128)S(1)}, f32[2,32,16,256]{3,2,1,0:T(8,128)S(1)}, u32[]{:S(2)}, u32[]{:S(2)}) %collective-permute-start.5) | collective-permute-done | bytes 1048608 | tf_op jit(solution)/shard_map/ppermute | solution.py:24
  377.2 7.3 collective-permute-start.6
  384.6 16.7 %collective-permute-done.6 = f32[2,32,16,256]{3,2,1,0:T(8,128)S(1)} collective-permute-done((f32[2,32,16,256]{3,2,1,0:T(8,128)S(1)}, f32[2,32,16,256]{3,2,1,0:T(8,128)S(1)}, u32[]{:S(2)}, u32[]{:S(2)}) %collective-permute-start.6) | collective-permute-done | bytes 1048608 | tf_op jit(solution)/shard_map/ppermute | solution.py:24
  409.9 13.5 %collective-permute-done.7 = f32[2,32,16,256]{3,2,1,0:T(8,128)} collective-permute-done((f32[2,32,16,256]{3,2,1,0:T(8,128)}, f32[2,32,16,256]{3,2,1,0:T(8,128)}, u32[]{:S(2)}, u32[]{:S(2)}) %collective-permute-start.7) | collective-permute-done | bytes 1048608 | tf_op jit(solution)/shard_map/ppermute | solution.py:24
  444.4 23.6 %collective-permute-done.10 = f32[2,32,16,256]{3,2,1,0:T(8,128)S(1)} collective-permute-done((f32[2,32,16,256]{3,2,1,0:T(8,128)S(1)}, f32[2,32,16,256]{3,2,1,0:T(8,128)S(1)}, u32[]{:S(2)}, u32[]{:S(2)}) %collective-permute-start.10) | collective-permute-done | bytes 1048608 | tf_op jit(solution)/shard_map/ppermute | solution.py:24
  473.0 22.6 %collective-permute-done.11 = f32[2,32,16,256]{3,2,1,0:T(8,128)S(1)} collective-permute-done((f32[2,32,16,256]{3,2,1,0:T(8,128)S(1)}, f32[2,32,16,256]{3,2,1,0:T(8,128)S(1)}, u32[]{:S(2)}, u32[]{:S(2)}) %collective-permute-start.11) | collective-permute-done | bytes 1048608 | tf_op jit(solution)/shard_map/ppermute | solution.py:24
  499.8 23.2 %collective-permute-done.12 = f32[2,32,16,256]{3,2,1,0:T(8,128)S(1)} collective-permute-done((f32[2,32,16,256]{3,2,1,0:T(8,128)S(1)}, f32[2,32,16,256]{3,2,1,0:T(8,128)S(1)}, u32[]{:S(2)}, u32[]{:S(2)}) %collective-permute-start.12) | collective-permute-done | bytes 1048608 | tf_op jit(solution)/shard_map/ppermute | solution.py:24
  528.5 21.3 %collective-permute-done.13 = f32[2,32,16,256]{3,2,1,0:T(8,128)S(1)} collective-permute-done((f32[2,32,16,256]{3,2,1,0:T(8,128)S(1)}, f32[2,32,16,256]{3,2,1,0:T(8,128)S(1)}, u32[]{:S(2)}, u32[]{:S(2)}) %collective-permute-start.13) | collective-permute-done | bytes 1048608 | tf_op jit(solution)/shard_map/ppermute | solution.py:24
  551.8 21.9 %collective-permute-done.14 = f32[2,32,16,256]{3,2,1,0:T(8,128)S(1)} collective-permute-done((f32[2,32,16,256]{3,2,1,0:T(8,128)S(1)}, f32[2,32,16,256]{3,2,1,0:T(8,128)S(1)}, u32[]{:S(2)}, u32[]{:S(2)}) %collective-permute-start.14) | collective-permute-done | bytes 1048608 | tf_op jit(solution)/shard_map/ppermute | solution.py:24
  575.5 21.7 %collective-permute-done.15 = f32[2,32,16,256]{3,2,1,0:T(8,128)S(1)} collective-permute-done((f32[2,32,16,256]{3,2,1,0:T(8,128)S(1)}, f32[2,32,16,256]{3,2,1,0:T(8,128)S(1)}, u32[]{:S(2)}, u32[]{:S(2)}) %collective-permute-start.15) | collective-permute-done | bytes 1048608 | tf_op jit(solution)/shard_map/ppermute | solution.py:24
  613.6 257.9 %while.38 = (s32[]{:T(128)}, f32[12,3,512]{2,1,0:T(4,128)S(1)}, f32[12,512]{1,0:T(8,128)}, f32[12,37,512]{2,1,0:T(8,128)}, f32[12,21,512]{2,1,0:T(8,128)}, /*ind...) while((s32[]{:T(128)}, f32[12,3,512]{2,1,0:T(4,128)S(1)}, ...), condition=%wide.region_10.11_spmd, body=%wide.region_6.10_spmd.sunk | while | flops 3670716416 | bytes 35318940 | solution.py:311
  623.3 8.8 fusion.383
  644.8 8.8 fusion.383
  666.3 8.8 fusion.383
  687.8 8.8 fusion.383
  709.3 8.8 fusion.383
  730.8 8.8 fusion.383
  752.3 8.8 fusion.383
  773.8 8.8 fusion.383
  795.3 8.8 fusion.383
  816.8 8.8 fusion.383
  838.2 8.8 fusion.383
  859.7 8.8 fusion.383
  872.3 7.2 all-to-all-start.1
  879.5 7.8 all-to-all-done.1
  (1080 shorter events, 477.1 us)
Async XLA Ops:
  7.1 15.3 %all-to-all-start = ((f32[16,3,5,128]{3,1,2,0:T(4,128)}), f32[16,3,5,128]{3,1,2,0:T(4,128)S(1)}, u32[]{:S(2)}, u32[]{:S(2)}) async-start(f32[16,3,5,128]{3,1,2,0:T(4,128)} %copy.88), calls=%async_computation | async-start | bytes 327680 | tf_op jit(solution)/shard_map/all_to_all | solution.py:216
  73.6 7.0 copy-start.15
  93.2 7.0 copy-start.15
  112.9 7.0 copy-start.15
  132.6 7.0 copy-start.15
  191.7 7.0 copy-start.15
  260.0 5.5 collective-permute-start
  265.6 10.0 %collective-permute-start.1 = (f32[32,5,256]{2,1,0:T(8,128)S(1)}, f32[32,5,256]{2,1,0:T(8,128)S(1)}, u32[]{:S(2)}, u32[]{:S(2)}) collective-permute-start(f32[32,5,256]{2,1,0:T(8,128)S(1)} %fusion.116), channel_id=1, source_target_pairs={{0,1},{1,2},{2,3},{3,4},{4,5},{5,6},{6,7},{7,8},{8,9},{9,10},{10,1... | collective-permute-start | bytes 491528 | tf_op jit(solution)/shard_map/ppermute | solution.py:30
  278.9 24.2 %collective-permute-start.2 = (f32[2,32,16,256]{3,2,1,0:T(8,128)S(1)}, f32[2,32,16,256]{3,2,1,0:T(8,128)S(1)}, u32[]{:S(2)}, u32[]{:S(2)}) collective-permute-start(f32[2,32,16,256]{3,2,1,0:T(8,128)S(1)} %pad_maximum_fusion), channel_id=1, source_target_pairs={{0,8},{8,0},{1,9},{9,1},{2,10},{10,2},{3,11},{11,3},{4,12},{12,4},... | collective-permute-start | bytes 3145736 | tf_op jit(solution)/shard_map/ppermute | solution.py:24
  304.7 22.1 %collective-permute-start.3 = (f32[2,32,16,256]{3,2,1,0:T(8,128)}, f32[2,32,16,256]{3,2,1,0:T(8,128)}, u32[]{:S(2)}, u32[]{:S(2)}) collective-permute-start(f32[2,32,16,256]{3,2,1,0:T(8,128)} %maximum_select_fusion), channel_id=1, source_target_pairs={{0,4},{4,0},{1,5},{5,1},{2,6},{6,2},{3,7},{7,3},{8,12},{12,8},{9,1... | collective-permute-start | bytes 3145736 | tf_op jit(solution)/shard_map/ppermute | solution.py:24
  304.9 23.7 %copy-start.6 = (f32[1,32,16,256]{3,2,1,0:T(8,128)S(1)}, f32[1,32,16,256]{3,2,1,0:T(8,128)}, u32[]{:S(2)}) copy-start(f32[1,32,16,256]{3,2,1,0:T(8,128)} %copy-done.5) | copy-start | bytes 1572868
  304.9 23.7 %copy-start.8 = (f32[1,32,16,256]{3,2,1,0:T(8,128)S(1)}, f32[1,32,16,256]{3,2,1,0:T(8,128)}, u32[]{:S(2)}) copy-start(f32[1,32,16,256]{3,2,1,0:T(8,128)} %copy-done.7) | copy-start | bytes 1572868
  330.4 25.6 %collective-permute-start.4 = (f32[2,32,16,256]{3,2,1,0:T(8,128)S(1)}, f32[2,32,16,256]{3,2,1,0:T(8,128)S(1)}, u32[]{:S(2)}, u32[]{:S(2)}) collective-permute-start(f32[2,32,16,256]{3,2,1,0:T(8,128)S(1)} %maximum_select_fusion.1), channel_id=1, source_target_pairs={{0,2},{2,0},{1,3},{3,1},{4,6},{6,4},{5,7},{7,5},{8,10},{10,8},{9,1... | collective-permute-start | bytes 3145736 | tf_op jit(solution)/shard_map/ppermute | solution.py:24
  356.6 17.2 %collective-permute-start.5 = (f32[2,32,16,256]{3,2,1,0:T(8,128)S(1)}, f32[2,32,16,256]{3,2,1,0:T(8,128)S(1)}, u32[]{:S(2)}, u32[]{:S(2)}) collective-permute-start(f32[2,32,16,256]{3,2,1,0:T(8,128)S(1)} %maximum_select_fusion.2), channel_id=1, source_target_pairs={{0,1},{1,0},{2,3},{3,2},{4,5},{5,4},{6,7},{7,6},{8,9},{9,8},{10,11... | collective-permute-start | bytes 3145736 | tf_op jit(solution)/shard_map/ppermute | solution.py:24
  377.2 24.1 %collective-permute-start.6 = (f32[2,32,16,256]{3,2,1,0:T(8,128)S(1)}, f32[2,32,16,256]{3,2,1,0:T(8,128)S(1)}, u32[]{:S(2)}, u32[]{:S(2)}) collective-permute-start(f32[2,32,16,256]{3,2,1,0:T(8,128)S(1)} %pad_maximum_fusion.1), channel_id=1, source_target_pairs={{0,64},{64,0},{16,80},{80,16},{32,96},{96,32},{48,112},{112,48},{1... | collective-permute-start | bytes 3145736 | tf_op jit(solution)/shard_map/ppermute | solution.py:24
  402.9 20.5 %collective-permute-start.7 = (f32[2,32,16,256]{3,2,1,0:T(8,128)}, f32[2,32,16,256]{3,2,1,0:T(8,128)}, u32[]{:S(2)}, u32[]{:S(2)}) collective-permute-start(f32[2,32,16,256]{3,2,1,0:T(8,128)} %maximum_select_fusion.4), channel_id=1, source_target_pairs={{0,32},{32,0},{16,48},{48,16},{64,96},{96,64},{80,112},{112,80},{1... | collective-permute-start | bytes 3145736 | tf_op jit(solution)/shard_map/ppermute | solution.py:24
  409.9 15.3 %copy-start.2 = (f32[1,32,16,256]{3,2,1,0:T(8,128)S(1)}, f32[1,32,16,256]{3,2,1,0:T(8,128)}, u32[]{:S(2)}) copy-start(f32[1,32,16,256]{3,2,1,0:T(8,128)} %copy-done.1) | copy-start | bytes 1572868
  409.9 15.3 %copy-start.4 = (f32[1,32,16,256]{3,2,1,0:T(8,128)S(1)}, f32[1,32,16,256]{3,2,1,0:T(8,128)}, u32[]{:S(2)}) copy-start(f32[1,32,16,256]{3,2,1,0:T(8,128)} %copy-done.3) | copy-start | bytes 1572868
  427.1 3.0 collective-permute-start.8
  439.1 2.7 collective-permute-start.9
  442.6 25.3 %collective-permute-start.10 = (f32[2,32,16,256]{3,2,1,0:T(8,128)S(1)}, f32[2,32,16,256]{3,2,1,0:T(8,128)S(1)}, u32[]{:S(2)}, u32[]{:S(2)}) collective-permute-start(f32[2,32,16,256]{3,2,1,0:T(8,128)S(1)} %maximum_select_fusion.8), channel_id=1, source_target_pairs={{0,32},{32,0},{16,48},{48,16},{64,96},{96,64},{80,112},{112,80},{1... | collective-permute-start | bytes 3145736 | tf_op jit(solution)/shard_map/ppermute | solution.py:24
  468.7 26.9 %collective-permute-start.11 = (f32[2,32,16,256]{3,2,1,0:T(8,128)S(1)}, f32[2,32,16,256]{3,2,1,0:T(8,128)S(1)}, u32[]{:S(2)}, u32[]{:S(2)}) collective-permute-start(f32[2,32,16,256]{3,2,1,0:T(8,128)S(1)} %maximum_select_fusion.9), channel_id=1, source_target_pairs={{0,64},{64,0},{16,80},{80,16},{32,96},{96,32},{48,112},{112,48},{1... | collective-permute-start | bytes 3145736 | tf_op jit(solution)/shard_map/ppermute | solution.py:24
  499.1 23.9 %collective-permute-start.12 = (f32[2,32,16,256]{3,2,1,0:T(8,128)S(1)}, f32[2,32,16,256]{3,2,1,0:T(8,128)S(1)}, u32[]{:S(2)}, u32[]{:S(2)}) collective-permute-start(f32[2,32,16,256]{3,2,1,0:T(8,128)S(1)} %maximum_select_fusion.10), channel_id=1, source_target_pairs={{0,1},{1,0},{2,3},{3,2},{4,5},{5,4},{6,7},{7,6},{8,9},{9,8},{10,11... | collective-permute-start | bytes 3145736 | tf_op jit(solution)/shard_map/ppermute | solution.py:24
  523.7 26.1 %collective-permute-start.13 = (f32[2,32,16,256]{3,2,1,0:T(8,128)S(1)}, f32[2,32,16,256]{3,2,1,0:T(8,128)S(1)}, u32[]{:S(2)}, u32[]{:S(2)}) collective-permute-start(f32[2,32,16,256]{3,2,1,0:T(8,128)S(1)} %maximum_select_fusion.11), channel_id=1, source_target_pairs={{0,2},{2,0},{1,3},{3,1},{4,6},{6,4},{5,7},{7,5},{8,10},{10,8},{9,1... | collective-permute-start | bytes 3145736 | tf_op jit(solution)/shard_map/ppermute | solution.py:24
  550.6 23.1 %collective-permute-start.14 = (f32[2,32,16,256]{3,2,1,0:T(8,128)S(1)}, f32[2,32,16,256]{3,2,1,0:T(8,128)S(1)}, u32[]{:S(2)}, u32[]{:S(2)}) collective-permute-start(f32[2,32,16,256]{3,2,1,0:T(8,128)S(1)} %maximum_select_fusion.12), channel_id=1, source_target_pairs={{0,4},{4,0},{1,5},{5,1},{2,6},{6,2},{3,7},{7,3},{8,12},{12,8},{9,1... | collective-permute-start | bytes 3145736 | tf_op jit(solution)/shard_map/ppermute | solution.py:24
  574.4 22.7 %collective-permute-start.15 = (f32[2,32,16,256]{3,2,1,0:T(8,128)S(1)}, f32[2,32,16,256]{3,2,1,0:T(8,128)S(1)}, u32[]{:S(2)}, u32[]{:S(2)}) collective-permute-start(f32[2,32,16,256]{3,2,1,0:T(8,128)S(1)} %maximum_select_fusion.13), channel_id=1, source_target_pairs={{0,8},{8,0},{1,9},{9,1},{2,10},{10,2},{3,11},{11,3},{4,12},{12,4},... | collective-permute-start | bytes 3145736 | tf_op jit(solution)/shard_map/ppermute | solution.py:24
  597.6 8.3 copy-start.26
  597.6 8.3 copy-start.30
  600.8 2.1 collective-permute-start.16
  602.9 9.6 %collective-permute-start.17 = (f32[37,5,256]{2,1,0:T(8,128)S(1)}, f32[37,5,256]{2,1,0:T(8,128)S(1)}, u32[]{:S(2)}, u32[]{:S(2)}) collective-permute-start(f32[37,5,256]{2,1,0:T(8,128)S(1)} %pad_maximum_fusion.3), channel_id=1, source_target_pairs={{0,15},{1,0},{2,1},{3,2},{4,3},{5,4},{6,5},{7,6},{8,7},{9,8},{10,9... | collective-permute-start | bytes 568328 | tf_op jit(solution)/shard_map/ppermute | solution.py:30
  613.6 274.4 %copy-start.28 = (f32[32]{0:T(128)S(1)}, f32[32]{0:T(128)}, u32[]{:S(2)}) copy-start(f32[32]{0:T(128)} %copy-done.27) | copy-start | bytes 388
  872.3 15.0 %all-to-all-start.1 = ((f32[16,3,3,128]{3,1,2,0:T(4,128)}), f32[16,3,3,128]{3,1,2,0:T(4,128)S(1)}, u32[]{:S(2)}, u32[]{:S(2)}) async-start(f32[16,3,3,128]{3,1,2,0:T(4,128)} %copy.106), calls=%async_computation.1 | async-start | bytes 196608 | tf_op jit(solution)/shard_map/all_to_all | solution.py:317
  (217 other events, 1166.9 us)
where the time goes:
time: 903 us; the launch traced here: 889 us
  waiting for transfers between devices  295 us (33%)
  other arithmetic  230 us (25%)
  matrix products  175 us (19%)
  local copies, waits for them, and re-layouts  136 us (15%)
  starting transfers between devices  46.7 us (5%)
    ppermute x14, waiting for transfers between devices, swapped(): return lax.ppermute(block, axis, route)  257 us
    dot_general x12, matrix products, pull(): sampled = jnp.einsum('cga,gz->caz', stacked, potential, precision=HIGHEST)  106 us
    dynamic_update_slice x72, other arithmetic, per_device(): extended, stored = lax.scan(deposit, start_grid, grouped)  84 us
    sub x144, other arithmetic, spline_six(): (older_values[k - 1] if k >= 1 else jnp.zeros_like(u)) - (older_values[k]...  58.4 us
    dot_general x12, matrix products, deposit(): jnp.dot(outer_table, table_z * group[3][:, None], precision=HIGHEST)  50.2 us
    mul x24, local copies, waits for them, and re-layouts, pull(): slope_x[:, None, :] * table_y[None, :, :]  42.3 us
    mul x12, other arithmetic, pull(): table_x[:, None, :] * table_y[None, :, :]  29.8 us
    ppermute x14, starting transfers between devices, swapped(): return lax.ppermute(block, axis, route)  28.7 us
  transfers between devices with their start and end apart: 20, of which 20 were waited for; matrix products, arithmetic and copies ran while one was open for 0% of the time, Pallas kernels for 0%

commit v1 on v0

--- a/solution.py
+++ b/solution.py
@@ -162,6 +162,33 @@
     return jnp.where(upper, turned, spectrum + partner)
 
 
+def complex_turn(apply_matrix, spectrum, mat_cos, mat_sin, inverse):
+    real_part, imag_part = (spectrum[0], spectrum[1])
+    sign = 1.0 if inverse else -1.0
+    return jnp.stack(
+        [
+            apply_matrix(mat_cos, real_part) - sign * apply_matrix(mat_sin, imag_part),
+            apply_matrix(mat_cos, imag_part) + sign * apply_matrix(mat_sin, real_part),
+        ]
+    )
+
+
+def transform_rows(spectrum, mat_cos, mat_sin, inverse):
+
+    def apply_matrix(matrix, values):
+        return jnp.einsum("sm,myz->syz", matrix, values, precision=HIGHEST)
+
+    return complex_turn(apply_matrix, spectrum, mat_cos, mat_sin, inverse)
+
+
+def transform_columns(spectrum, mat_cos, mat_sin, inverse):
+
+    def apply_matrix(matrix, values):
+        return jnp.einsum("sm,xmz->xsz", matrix, values, precision=HIGHEST)
+
+    return complex_turn(apply_matrix, spectrum, mat_cos, mat_sin, inverse)
+
+
 def place_table(base, values, span):
     atoms_count = base.shape[0]
     slots_index = jnp.arange(span, dtype=jnp.int32)[:, None]
@@ -257,31 +284,23 @@
     ).reshape(2, span_x, span_y, K)
     index_x = lax.axis_index("px")
     index_y = lax.axis_index("py")
-    bits_x = rows_dev.bit_length() - 1
-    bits_y = cols_dev.bit_length() - 1
-    start_x = reverse_bits(index_x, bits_x)
-    start_y = reverse_bits(index_y, bits_y)
-    for bit_number in reversed(range(bits_y)):
-        spectrum = butterfly_section(spectrum, index_y, bit_number, False, swap_columns)
-    column_cos, column_sin = local_forward(start_y, span_y, cols_dev)
-    spectrum = mix_columns(spectrum, column_cos, column_sin)
-    wave_y = start_y + cols_dev * jnp.arange(span_y, dtype=jnp.int32)
-    wave_z = jnp.arange(K, dtype=jnp.int32)
-    for bit_number in reversed(range(bits_x)):
-        spectrum = butterfly_section(spectrum, index_x, bit_number, False, swap_rows)
-    row_cos, row_sin = local_forward(start_x, span_x, rows_dev)
-    spectrum = mix_rows(spectrum, row_cos, row_sin)
-    wave_x = start_x + rows_dev * jnp.arange(span_x, dtype=jnp.int32)
+    spectrum = lax.all_to_all(spectrum, "py", split_axis=3, concat_axis=2, tiled=True)
+    spectrum = transform_columns(spectrum, depth_cos, depth_sin, False)
+    spectrum = lax.all_to_all(spectrum, "px", split_axis=2, concat_axis=1, tiled=True)
+    spectrum = transform_rows(spectrum, depth_cos, depth_sin, False)
+    span_ky = K // rows_dev
+    span_kz = K // cols_dev
+    wave_x = jnp.arange(K, dtype=jnp.int32)
+    wave_y = index_x * span_ky + jnp.arange(span_ky, dtype=jnp.int32)
+    wave_z = index_y * span_kz + jnp.arange(span_kz, dtype=jnp.int32)
     kernel = influence(wave_x[:, None, None], wave_y[None, :, None], wave_z[None, None, :], K) * (
         1.0 / float(K**3)
     )
     spectrum = spectrum * kernel[None]
-    spectrum = mix_rows(spectrum, row_cos.T, -row_sin.T)
-    for bit_number in range(bits_x):
-        spectrum = butterfly_section(spectrum, index_x, bit_number, True, swap_rows)
-    spectrum = mix_columns(spectrum, column_cos.T, -column_sin.T)
-    for bit_number in range(bits_y):
-        spectrum = butterfly_section(spectrum, index_y, bit_number, True, swap_columns)
+    spectrum = transform_rows(spectrum, depth_cos, depth_sin, True)
+    spectrum = lax.all_to_all(spectrum, "px", split_axis=1, concat_axis=2, tiled=True)
+    spectrum = transform_columns(spectrum, depth_cos, depth_sin, True)
+    spectrum = lax.all_to_all(spectrum, "py", split_axis=2, concat_axis=3, tiled=True)
     real_flat = spectrum[0].reshape(span_x * span_y, K)
     imag_flat = spectrum[1].reshape(span_x * span_y, K)
     potential = (

time: 903 us -> 804 us (0.89)
  waiting for transfers between devices: 295 us -> 55.5 us
  local copies, waits for them, and re-layouts: 136 us -> 233 us
  blocking collectives: 0 us -> 56.5 us
  starting transfers between devices: 46.7 us -> 21 us
  matrix products: 175 us -> 195 us
    ppermute x14 -> x0, waiting for transfers between devices: 257 us -> none  [swapped(): return lax.ppermute(block, axis, route)]
    all_to_all x0 -> x3, blocking collectives: none -> 56.5 us  [the longest x1 19.9 us: per_device(): lax.all_to_all(spectrum, 'py', split_axis=2, concat_axis=3, tiled=True)]
    ppermute x14 -> x0, starting transfers between devices: 28.7 us -> none  [swapped(): return lax.ppermute(block, axis, route)]
    unnamed x27 -> x19, local copies, waits for them, and re-layouts: 0.89 us -> 29.4 us
    another operation x0 -> x6, local copies, waits for them, and re-layouts: none -> 24.5 us  [the longest x3 13.2 us: complex_turn(): jnp.stack([apply_matrix(mat_cos, real_part) - sign * apply_matrix(mat_sin...]
    all_to_all x0 -> x5, local copies, waits for them, and re-layouts: none -> 16.9 us  [the longest x2 5.19 us: per_device(): lax.all_to_all(spectrum, 'py', split_axis=3, concat_axis=2, tiled=True)]
    all_to_all x0 -> x1, waiting for transfers between devices: none -> 15.2 us  [per_device(): lax.all_to_all(spectrum, 'px', split_axis=2, concat_axis=1, tiled=True)]
    slice x0 -> x7, local copies, waits for them, and re-layouts: none -> 13.2 us  [the longest x5 7.13 us: complex_turn(): real_part, imag_part = (spectrum[0], spectrum[1])]
  transfers between devices with their start and end apart: 20 -> 7, of which waited for: 20 -> 7; matrix products, arithmetic and copies ran while one was open for 0% -> 0% of each run, Pallas kernels for 0% -> 0%
where the time goes in v1:
time: 804 us; the launch traced here: 790 us
  local copies, waits for them, and re-layouts  233 us (29%)
  other arithmetic  224 us (28%)
  matrix products  195 us (24%)
  blocking collectives  56.5 us (7%)
  waiting for transfers between devices  55.5 us (7%)
  starting transfers between devices  21 us (3%)
    dot_general x12, matrix products, pull(): sampled = jnp.einsum('cga,gz->caz', stacked, potential, precision=HIGHEST)  106 us
    dynamic_update_slice x72, other arithmetic, per_device(): extended, stored = lax.scan(deposit, start_grid, grouped)  83.7 us
    sub x144, other arithmetic, spline_six(): (older_values[k - 1] if k >= 1 else jnp.zeros_like(u)) - (older_values[k]...  57.3 us
    dot_general x12, matrix products, deposit(): jnp.dot(outer_table, table_z * group[3][:, None], precision=HIGHEST)  50.5 us
    mul x24, local copies, waits for them, and re-layouts, pull(): slope_x[:, None, :] * table_y[None, :, :]  42.5 us
    mul x12, other arithmetic, pull(): table_x[:, None, :] * table_y[None, :, :]  30.4 us
    unnamed x19, local copies, waits for them, and re-layouts  29.4 us
    mul x24, local copies, waits for them, and re-layouts, pull(): table_x[:, None, :] * slope_y[None, :, :]  28.4 us
  transfers between devices with their start and end apart: 7, of which 7 were waited for; matrix products, arithmetic and copies ran while one was open for 0% of the time, Pallas kernels for 0%

profile of v1, /device:TPU:0, one launch (start us, length us, event | category | flops | bytes accessed | tf_op | source)
XLA Modules:
  0.0 790.2 jit_solution(15784062410698012979)
XLA Ops:
  7.1 7.1 all-to-all-start
  14.3 8.1 %all-to-all-done = f32[16,3,5,128]{3,1,2,0:T(4,128)S(1)} async-done(((f32[16,3,5,128]{3,1,2,0:T(4,128)}), f32[16,3,5,128]{3,1,2,0:T(4,128)S(1)}, u32[]{:S(2)}, u32[]{:S(2)}) %all-to-all-start) | async-done | bytes 122912 | tf_op jit(solution)/shard_map/all_to_all | solution.py:243
  23.3 234.4 %while.39 = (s32[]{:T(128)}, f32[777,256]{1,0:T(8,128)}, f32[12,37,512]{2,1,0:T(8,128)}, f32[12,37,512]{2,1,0:T(8,128)}, f32[12,21,512]{2,1,0:T(8,128)}, /*index...) while((s32[]{:T(128)}, f32[777,256]{1,0:T(8,128)}, ...), condition=%wide.region_5.6_spmd.clone, body=%wide.region_4.5_spmd.clone.sunk | while | flops 1231531008 | bytes 10090179 | solution.py:271
  264.8 9.4 %collective-permute-done.1 = f32[32,5,256]{2,1,0:T(8,128)S(1)} collective-permute-done((f32[32,5,256]{2,1,0:T(8,128)S(1)}, f32[32,5,256]{2,1,0:T(8,128)S(1)}, u32[]{:S(2)}, u32[]{:S(2)}) %collective-permute-start.1) | collective-permute-done | bytes 163872 | tf_op jit(solution)/shard_map/ppermute | solution.py:30
  277.5 4.4 copy.122
  285.8 18.2 %all_to_all.70 = f32[16,1,16384]{2,1,0:T(1,128)S(1)} all-to-all(f32[16,1,16384]{2,1,0:T(1,128)S(1)} %reshape.4691), channel_id=1, replica_groups=mesh['px'=8,'py'=16] {'py'}, dimensions={0} | all-to-all | bytes 2097152 | tf_op jit(solution)/shard_map/all_to_all | solution.py:287
  310.4 4.6 copy.123
  329.6 4.4 copy.130
  334.0 4.8 reshape.4693
  338.8 5.8 all-to-all-start.2
  345.4 15.2 %all-to-all-done.2 = f32[8,1,32768]{2,1,0:T(1,128)S(1)} async-done(((f32[8,1,32768]{2,1,0:T(1,128)}), f32[8,1,32768]{2,1,0:T(1,128)S(1)}, u32[]{:S(2)}, u32[]{:S(2)}) %all-to-all-start.2) | async-done | bytes 1048608 | tf_op jit(solution)/shard_map/all_to_all | solution.py:289
  367.0 4.6 copy.163
  401.9 18.4 %all_to_all.71 = f32[8,1,32768]{2,1,0:T(1,128)S(1)} all-to-all(f32[8,1,32768]{2,1,0:T(1,128)S(1)} %reshape.4695), channel_id=1, replica_groups=mesh['px'=8,'py'=16] {'px'}, dimensions={0} | all-to-all | bytes 2097152 | tf_op jit(solution)/shard_map/all_to_all | solution.py:301
  426.7 4.6 copy.162
  452.4 19.9 %all_to_all.72 = f32[16,1,16384]{2,1,0:T(1,128)S(1)} all-to-all(f32[16,1,16384]{2,1,0:T(1,128)S(1)} %reshape.4697), channel_id=1, replica_groups=mesh['px'=8,'py'=16] {'py'}, dimensions={0} | all-to-all | bytes 2097152 | tf_op jit(solution)/shard_map/all_to_all | solution.py:303
  482.5 5.4 copy.136
  506.0 8.7 %collective-permute-done.3 = f32[37,5,256]{2,1,0:T(8,128)S(1)} collective-permute-done((f32[37,5,256]{2,1,0:T(8,128)S(1)}, f32[37,5,256]{2,1,0:T(8,128)S(1)}, u32[]{:S(2)}, u32[]{:S(2)}) %collective-permute-start.3) | collective-permute-done | bytes 189472 | tf_op jit(solution)/shard_map/ppermute | solution.py:30
  515.9 258.1 %while.38 = (s32[]{:T(128)}, f32[12,3,512]{2,1,0:T(4,128)S(1)}, f32[12,512]{1,0:T(8,128)}, f32[12,37,512]{2,1,0:T(8,128)}, f32[12,21,512]{2,1,0:T(8,128)}, /*ind...) while((s32[]{:T(128)}, f32[12,3,512]{2,1,0:T(4,128)S(1)}, ...), condition=%wide.region_10.11_spmd, body=%wide.region_6.10_spmd.sunk | while | flops 3670716416 | bytes 35318940 | solution.py:330
  525.7 8.8 %fusion.345 = f32[3,512,256]{1,2,0:T(8,128)} fusion(f32[1,777,512]{2,1,0:T(8,128)S(1)} %mul.7878, f32[1,777,512]{2,1,0:T(8,128)} %mul.7879, f32[1,777,512]{2,1,0:T(8,128)} %mul.7880, f32[777,256]{1,0:T(8,128)} %get-tuple-element.902), kind=kOutput, calls=%fused_computation.2.clone.1 | convolution fusion | flops 3668732928 | bytes 7142400 | tf_op jit(solution)/shard_map/while/body/eval_jaxpr/cga,gz->caz/dot_general | solution.py:324
  547.2 8.8 %fusion.345 = f32[3,512,256]{1,2,0:T(8,128)} fusion(f32[1,777,512]{2,1,0:T(8,128)S(1)} %mul.7878, f32[1,777,512]{2,1,0:T(8,128)} %mul.7879, f32[1,777,512]{2,1,0:T(8,128)} %mul.7880, f32[777,256]{1,0:T(8,128)} %get-tuple-element.902), kind=kOutput, calls=%fused_computation.2.clone.1 | convolution fusion | flops 3668732928 | bytes 7142400 | tf_op jit(solution)/shard_map/while/body/eval_jaxpr/cga,gz->caz/dot_general | solution.py:324
  568.7 8.8 %fusion.345 = f32[3,512,256]{1,2,0:T(8,128)} fusion(f32[1,777,512]{2,1,0:T(8,128)S(1)} %mul.7878, f32[1,777,512]{2,1,0:T(8,128)} %mul.7879, f32[1,777,512]{2,1,0:T(8,128)} %mul.7880, f32[777,256]{1,0:T(8,128)} %get-tuple-element.902), kind=kOutput, calls=%fused_computation.2.clone.1 | convolution fusion | flops 3668732928 | bytes 7142400 | tf_op jit(solution)/shard_map/while/body/eval_jaxpr/cga,gz->caz/dot_general | solution.py:324
  590.2 8.8 %fusion.345 = f32[3,512,256]{1,2,0:T(8,128)} fusion(f32[1,777,512]{2,1,0:T(8,128)S(1)} %mul.7878, f32[1,777,512]{2,1,0:T(8,128)} %mul.7879, f32[1,777,512]{2,1,0:T(8,128)} %mul.7880, f32[777,256]{1,0:T(8,128)} %get-tuple-element.902), kind=kOutput, calls=%fused_computation.2.clone.1 | convolution fusion | flops 3668732928 | bytes 7142400 | tf_op jit(solution)/shard_map/while/body/eval_jaxpr/cga,gz->caz/dot_general | solution.py:324
  611.7 8.8 %fusion.345 = f32[3,512,256]{1,2,0:T(8,128)} fusion(f32[1,777,512]{2,1,0:T(8,128)S(1)} %mul.7878, f32[1,777,512]{2,1,0:T(8,128)} %mul.7879, f32[1,777,512]{2,1,0:T(8,128)} %mul.7880, f32[777,256]{1,0:T(8,128)} %get-tuple-element.902), kind=kOutput, calls=%fused_computation.2.clone.1 | convolution fusion | flops 3668732928 | bytes 7142400 | tf_op jit(solution)/shard_map/while/body/eval_jaxpr/cga,gz->caz/dot_general | solution.py:324
  633.2 8.8 %fusion.345 = f32[3,512,256]{1,2,0:T(8,128)} fusion(f32[1,777,512]{2,1,0:T(8,128)S(1)} %mul.7878, f32[1,777,512]{2,1,0:T(8,128)} %mul.7879, f32[1,777,512]{2,1,0:T(8,128)} %mul.7880, f32[777,256]{1,0:T(8,128)} %get-tuple-element.902), kind=kOutput, calls=%fused_computation.2.clone.1 | convolution fusion | flops 3668732928 | bytes 7142400 | tf_op jit(solution)/shard_map/while/body/eval_jaxpr/cga,gz->caz/dot_general | solution.py:324
  654.7 8.8 %fusion.345 = f32[3,512,256]{1,2,0:T(8,128)} fusion(f32[1,777,512]{2,1,0:T(8,128)S(1)} %mul.7878, f32[1,777,512]{2,1,0:T(8,128)} %mul.7879, f32[1,777,512]{2,1,0:T(8,128)} %mul.7880, f32[777,256]{1,0:T(8,128)} %get-tuple-element.902), kind=kOutput, calls=%fused_computation.2.clone.1 | convolution fusion | flops 3668732928 | bytes 7142400 | tf_op jit(solution)/shard_map/while/body/eval_jaxpr/cga,gz->caz/dot_general | solution.py:324
  676.2 8.8 %fusion.345 = f32[3,512,256]{1,2,0:T(8,128)} fusion(f32[1,777,512]{2,1,0:T(8,128)S(1)} %mul.7878, f32[1,777,512]{2,1,0:T(8,128)} %mul.7879, f32[1,777,512]{2,1,0:T(8,128)} %mul.7880, f32[777,256]{1,0:T(8,128)} %get-tuple-element.902), kind=kOutput, calls=%fused_computation.2.clone.1 | convolution fusion | flops 3668732928 | bytes 7142400 | tf_op jit(solution)/shard_map/while/body/eval_jaxpr/cga,gz->caz/dot_general | solution.py:324
  697.7 8.8 %fusion.345 = f32[3,512,256]{1,2,0:T(8,128)} fusion(f32[1,777,512]{2,1,0:T(8,128)S(1)} %mul.7878, f32[1,777,512]{2,1,0:T(8,128)} %mul.7879, f32[1,777,512]{2,1,0:T(8,128)} %mul.7880, f32[777,256]{1,0:T(8,128)} %get-tuple-element.902), kind=kOutput, calls=%fused_computation.2.clone.1 | convolution fusion | flops 3668732928 | bytes 7142400 | tf_op jit(solution)/shard_map/while/body/eval_jaxpr/cga,gz->caz/dot_general | solution.py:324
  719.2 8.8 %fusion.345 = f32[3,512,256]{1,2,0:T(8,128)} fusion(f32[1,777,512]{2,1,0:T(8,128)S(1)} %mul.7878, f32[1,777,512]{2,1,0:T(8,128)} %mul.7879, f32[1,777,512]{2,1,0:T(8,128)} %mul.7880, f32[777,256]{1,0:T(8,128)} %get-tuple-element.902), kind=kOutput, calls=%fused_computation.2.clone.1 | convolution fusion | flops 3668732928 | bytes 7142400 | tf_op jit(solution)/shard_map/while/body/eval_jaxpr/cga,gz->caz/dot_general | solution.py:324
  740.7 8.8 %fusion.345 = f32[3,512,256]{1,2,0:T(8,128)} fusion(f32[1,777,512]{2,1,0:T(8,128)S(1)} %mul.7878, f32[1,777,512]{2,1,0:T(8,128)} %mul.7879, f32[1,777,512]{2,1,0:T(8,128)} %mul.7880, f32[777,256]{1,0:T(8,128)} %get-tuple-element.902), kind=kOutput, calls=%fused_computation.2.clone.1 | convolution fusion | flops 3668732928 | bytes 7142400 | tf_op jit(solution)/shard_map/while/body/eval_jaxpr/cga,gz->caz/dot_general | solution.py:324
  762.3 8.8 %fusion.345 = f32[3,512,256]{1,2,0:T(8,128)} fusion(f32[1,777,512]{2,1,0:T(8,128)S(1)} %mul.7878, f32[1,777,512]{2,1,0:T(8,128)} %mul.7879, f32[1,777,512]{2,1,0:T(8,128)} %mul.7880, f32[777,256]{1,0:T(8,128)} %get-tuple-element.902), kind=kOutput, calls=%fused_computation.2.clone.1 | convolution fusion | flops 3668732928 | bytes 7142400 | tf_op jit(solution)/shard_map/while/body/eval_jaxpr/cga,gz->caz/dot_general | solution.py:324
  774.7 5.9 all-to-all-start.5
  780.6 7.8 all-to-all-done.5
  (1042 shorter events, 521.7 us)
Async XLA Ops:
  7.1 15.3 %all-to-all-start = ((f32[16,3,5,128]{3,1,2,0:T(4,128)}), f32[16,3,5,128]{3,1,2,0:T(4,128)S(1)}, u32[]{:S(2)}, u32[]{:S(2)}) async-start(f32[16,3,5,128]{3,1,2,0:T(4,128)} %copy.119), calls=%async_computation | async-start | bytes 327680 | tf_op jit(solution)/shard_map/all_to_all | solution.py:243
  24.7 6.7 copy-start.3
  24.7 6.7 copy-start.4
  43.9 6.7 copy-start.3
  53.6 7.0 copy-start.7
  63.4 6.7 copy-start.3
  63.4 6.7 copy-start.4
  73.2 7.0 copy-start.7
  83.0 6.7 copy-start.3
  83.0 6.7 copy-start.4
  92.8 7.0 copy-start.7
  102.6 6.7 copy-start.3
  112.3 7.0 copy-start.7
  122.2 6.7 copy-start.3
  131.9 7.0 copy-start.7
  151.5 7.0 copy-start.7
  161.3 6.7 copy-start.3
  161.3 6.7 copy-start.4
  171.0 7.0 copy-start.7
  190.6 7.0 copy-start.7
  210.2 7.0 copy-start.7
  229.7 7.0 copy-start.7
  239.5 6.7 copy-start.3
  239.5 6.7 copy-start.4
  249.3 7.0 copy-start.7
  258.6 5.5 collective-permute-start
  264.2 10.0 %collective-permute-start.1 = (f32[32,5,256]{2,1,0:T(8,128)S(1)}, f32[32,5,256]{2,1,0:T(8,128)S(1)}, u32[]{:S(2)}, u32[]{:S(2)}) collective-permute-start(f32[32,5,256]{2,1,0:T(8,128)S(1)} %fusion.109), channel_id=1, source_target_pairs={{0,1},{1,2},{2,3},{3,4},{4,5},{5,6},{6,7},{7,8},{8,9},{9,10},{10,1... | collective-permute-start | bytes 491528 | tf_op jit(solution)/shard_map/ppermute | solution.py:30
  338.8 21.7 %all-to-all-start.2 = ((f32[8,1,32768]{2,1,0:T(1,128)}), f32[8,1,32768]{2,1,0:T(1,128)S(1)}, u32[]{:S(2)}, u32[]{:S(2)}) async-start(f32[8,1,32768]{2,1,0:T(1,128)} %reshape.4693), calls=%async_computation.2 | async-start | bytes 2097152 | tf_op jit(solution)/shard_map/all_to_all | solution.py:289
  502.4 2.1 collective-permute-start.2
  504.5 10.2 %collective-permute-start.3 = (f32[37,5,256]{2,1,0:T(8,128)S(1)}, f32[37,5,256]{2,1,0:T(8,128)S(1)}, u32[]{:S(2)}, u32[]{:S(2)}) collective-permute-start(f32[37,5,256]{2,1,0:T(8,128)S(1)} %pad_maximum_fusion.5), channel_id=1, source_target_pairs={{0,15},{1,0},{2,1},{3,2},{4,3},{5,4},{6,5},{7,6},{8,7},{9,8},{10,9... | collective-permute-start | bytes 568328 | tf_op jit(solution)/shard_map/ppermute | solution.py:30
  515.9 273.2 %copy-start.20 = (f32[32]{0:T(128)S(1)}, f32[32]{0:T(128)}, u32[]{:S(2)}) copy-start(f32[32]{0:T(128)} %copy-done.19) | copy-start | bytes 388
  774.7 13.7 %all-to-all-start.5 = ((f32[16,3,3,128]{3,1,2,0:T(4,128)}), f32[16,3,3,128]{3,1,2,0:T(4,128)S(1)}, u32[]{:S(2)}, u32[]{:S(2)}) async-start(f32[16,3,3,128]{3,1,2,0:T(4,128)} %copy.141), calls=%async_computation.5 | async-start | bytes 196608 | tf_op jit(solution)/shard_map/all_to_all | solution.py:336
  (196 other events, 1043.0 us)
